TPU v7x, 32 devices: a whole 2x2x4 slice. The times are simulated.
32 devices in a mesh: seq: 8 (over y, x, core), head: 4 (over z).
Axes of the slice: x: 2, y: 2, z: 4, core: 2. Of those that a mesh axis runs over, the one named last changes fastest.
Arguments:
- query_rows: bfloat16 [1024, 2304], P(('seq', 'head')), may hold values from -6 to 6
- key_rows: bfloat16 [1024, 2304], P(('seq', 'head')), may hold values from -6 to 6
- value_rows: bfloat16 [1024, 2304], P(('seq', 'head')), may hold values from -6 to 6
- residual_in: bfloat16 [1024, 2304], P(('seq', 'head')), may hold values from -40 to 40
- norm_gain: float32 [2304], replicated, may hold values from 0.1 to 1.9
- router_weight: bfloat16 [2304, 8], replicated, may hold values from -0.125 to 0.125
- segment_ids: int32 [1024], P('seq'), may hold values from 0 to 3, never falling along the last dimension, each value on 1 to 897 neighbouring positions
- expert_ids: int32 [1024, 2], P(('seq', 'head')), may hold values from 0 to 7, all different within a row; in each aligned block of 32 rows (0 to 31, 32 to 63, ...) at most 9 rows name the same one
- gate_weight: bfloat16 [2304, 23040], P(None, ('seq', 'head')), may hold values from -0.125 to 0.125
- up_weight: bfloat16 [2304, 23040], P(None, ('seq', 'head')), may hold values from -0.125 to 0.125
- down_weight: bfloat16 [2304, 23040], P(None, ('seq', 'head')), may hold values from -0.109375 to 0.109375
- out_weight: bfloat16 [2304, 2304], P('head'), may hold values from -0.125 to 0.125
Outputs:
- residual_out: bfloat16 [1024, 2304], P(('seq', 'head'))
- key_cache: bfloat16 [1024, 2304], P('seq', 'head')
- value_cache: bfloat16 [1024, 2304], P('seq', 'head')
Inputs may be any that keep to these rules, and one draw needn't show every extreme that they name: `segment_ids`: each segment covers at most 897 tokens. `expert_ids`: in the rows of one device no expert is named more than 9 times.
All inputs are finite; a program needn't handle non-finite values.
Results may differ from a plain program's by a relative error of at most 0.005.
Values may be sent and summed in bfloat16 or wider, within the bound.
No kernel may reach another device: no remote copies, remote signals or barrier semaphores. Data moves between devices by JAX's collectives and lax.ppermute only.
A program may use at most 128 MiB of HBM per device.

v0:
```python
import math
import jax
import jax.numpy as jnp
from jax import lax
from jax.sharding import PartitionSpec as P

D = 2304
HDIM = 64
LEVELS = 4
CAP = 9
residual_scale = 1.4 / math.sqrt(40.0)
norm_epsilon = 1e-05


def passed_along(value, axis, by):
    length = lax.axis_size(axis)
    pairs = [(i, i + by) for i in range(length) if 0 <= i + by < length]
    return lax.ppermute(value, axis, pairs)


def score_piece(queries, key_piece, piece_allowed):
    raw_scores = jnp.einsum(
        "qhd,khd->hqk", queries, key_piece, preferred_element_type=jnp.float32
    ) * queries.shape[2] ** (-0.5)
    return jnp.where(piece_allowed[None], raw_scores, -jnp.inf)


def mix_piece(rounded_piece, value_piece):
    return jnp.einsum(
        "hqk,khd->qhd", rounded_piece, value_piece, preferred_element_type=jnp.float32
    )


def per_device(
    query_rows,
    key_rows,
    value_rows,
    residual_in,
    norm_gain,
    router_weight,
    segment_ids,
    expert_ids,
    gate_weight,
    up_weight,
    down_weight,
    out_weight,
):
    head_count = lax.axis_size("head")
    seq_count = lax.axis_size("seq")
    tok_local = query_rows.shape[0]
    group_width = query_rows.shape[1] // head_count
    heads_here = group_width // HDIM
    stretch_len = tok_local * head_count
    span_count = min(2**LEVELS * 32 // tok_local, seq_count)
    gate_full, up_full, down_full = (
        lax.all_gather(gate_weight, "head", axis=1, tiled=True),
        lax.all_gather(up_weight, "head", axis=1, tiled=True),
        lax.all_gather(down_weight, "head", axis=1, tiled=True),
    )
    expert_count = router_weight.shape[1]
    replicas = seq_count // expert_count
    seq_place = lax.axis_index("seq")
    query_head, key_head, value_head = (
        lax.all_to_all(
            query_rows.reshape(tok_local, head_count, group_width),
            "head",
            split_axis=1,
            concat_axis=0,
            tiled=True,
        ),
        lax.all_to_all(
            key_rows.reshape(tok_local, head_count, group_width),
            "head",
            split_axis=1,
            concat_axis=0,
            tiled=True,
        ),
        lax.all_to_all(
            value_rows.reshape(tok_local, head_count, group_width),
            "head",
            split_axis=1,
            concat_axis=0,
            tiled=True,
        ),
    )
    query_head = query_head.reshape(stretch_len, group_width)
    key_head = key_head.reshape(stretch_len, group_width)
    value_head = value_head.reshape(stretch_len, group_width)
    front_rows = (span_count - 1) * stretch_len
    key_window = jnp.concatenate((jnp.zeros((front_rows, group_width), jnp.bfloat16), key_head), 0)
    value_window = jnp.concatenate(
        (jnp.zeros((front_rows, group_width), jnp.bfloat16), value_head), 0
    )
    segment_window = jnp.concatenate((jnp.zeros((front_rows,), jnp.int32), segment_ids), 0)

    def advance(step_index, carried):
        moving, keys_held, values_held, segments_held = carried
        moving = passed_along((moving[0], moving[1], moving[2]), "seq", 1)
        write_place = (span_count - 1 - step_index) * stretch_len
        keys_held = lax.dynamic_update_slice_in_dim(keys_held, moving[0], write_place, 0)
        values_held = lax.dynamic_update_slice_in_dim(values_held, moving[1], write_place, 0)
        segments_held = lax.dynamic_update_slice_in_dim(segments_held, moving[2], write_place, 0)
        return (moving, keys_held, values_held, segments_held)

    moving_final, key_window, value_window, segment_window = lax.fori_loop(
        1,
        span_count,
        advance,
        ((key_head, value_head, segment_ids), key_window, value_window, segment_window),
    )
    key_total = span_count * stretch_len
    query_place = seq_place * stretch_len + jnp.arange(stretch_len, dtype=jnp.int32)
    key_place = (seq_place - span_count + 1) * stretch_len + jnp.arange(key_total, dtype=jnp.int32)
    allowed = (
        (segment_window[None, :] == segment_ids[:, None])
        & (key_place[None, :] <= query_place[:, None])
        & (key_place[None, :] >= 0)
    )
    queries = query_head.reshape(stretch_len, heads_here, HDIM)
    keys_all = key_window.reshape(key_total, heads_here, HDIM)
    values_all = value_window.reshape(key_total, heads_here, HDIM)
    masked = score_piece(queries, keys_all, allowed)
    row_max = jnp.max(masked, -1, keepdims=True)
    weights = jnp.where(allowed[None], jnp.exp(masked - row_max), 0.0)
    totals = jnp.sum(weights, -1)
    mixture = mix_piece(weights.astype(jnp.bfloat16), values_all)
    attention = (
        (mixture / jnp.transpose(totals)[:, :, None])
        .astype(jnp.bfloat16)
        .reshape(stretch_len, group_width)
    )
    attended_sum = lax.psum_scatter(
        jnp.dot(attention, out_weight, preferred_element_type=jnp.float32).astype(jnp.bfloat16),
        "head",
        scatter_dimension=0,
        tiled=True,
    ).astype(jnp.float32)
    middle = (residual_in.astype(jnp.float32) + residual_scale * attended_sum).astype(jnp.bfloat16)
    middle_wide = middle.astype(jnp.float32)
    mean_square = jnp.mean(middle_wide * middle_wide, -1, keepdims=True)
    normed = (middle_wide * lax.rsqrt(mean_square + norm_epsilon) * norm_gain).astype(jnp.bfloat16)
    route_count = expert_ids.shape[1]
    logits = jnp.dot(normed, router_weight, preferred_element_type=jnp.float32)
    route_hot = expert_ids[:, :, None] == jnp.arange(expert_count, dtype=jnp.int32)[None, None, :]
    chosen = jnp.sum(jnp.where(route_hot, logits[:, None, :], 0.0), -1)
    first_weight = 1.0 / (1.0 + jnp.exp(chosen[:, 1] - chosen[:, 0]))
    second_weight = 1.0 / (1.0 + jnp.exp(chosen[:, 0] - chosen[:, 1]))
    flat_hot = route_hot.reshape(tok_local * route_count, expert_count).astype(jnp.int32)
    before_count = jnp.cumsum(flat_hot, 0) - flat_hot
    route_rank = jnp.sum(before_count * flat_hot, -1)
    slot_ids = (expert_ids.reshape(-1) * CAP + route_rank).reshape(tok_local, route_count)
    slot_total = expert_count * CAP
    dispatch = jnp.any(
        slot_ids[None, :, :] == jnp.arange(slot_total, dtype=jnp.int32)[:, None, None], -1
    ).astype(jnp.bfloat16)
    packed = (
        jnp.dot(dispatch, normed, preferred_element_type=jnp.float32)
        .astype(jnp.bfloat16)
        .reshape(expert_count, CAP, D)
    )
    outgoing = jnp.broadcast_to(packed[:, None], (expert_count, replicas, CAP, D)).reshape(
        seq_count, CAP, D
    )
    arrived = lax.all_to_all(outgoing, "seq", split_axis=0, concat_axis=0, tiled=True)
    slot_count = arrived.shape[1]
    flat_rows = arrived.reshape(seq_count * slot_count, D)
    gate_act = jnp.dot(flat_rows, gate_full, preferred_element_type=jnp.float32)
    up_act = jnp.dot(flat_rows, up_full, preferred_element_type=jnp.float32)
    hidden = (jax.nn.silu(gate_act) * up_act).astype(jnp.bfloat16)
    shard_out = lax.dot_general(
        hidden, down_full, (((1,), (1,)), ((), ())), preferred_element_type=jnp.float32
    ).astype(jnp.bfloat16)
    returned = lax.all_to_all(
        shard_out.reshape(seq_count, slot_count, D), "seq", split_axis=0, concat_axis=0, tiled=True
    )
    expert_out = jnp.sum(
        returned.reshape(expert_count, replicas, CAP, D).astype(jnp.float32), 1
    ).reshape(slot_total, D)
    first_rows = expert_out[slot_ids[:, 0]]
    second_rows = expert_out[slot_ids[:, 1]]
    moe_sum = first_weight[:, None] * first_rows + second_weight[:, None] * second_rows
    residual_out = (middle_wide + residual_scale * moe_sum).astype(jnp.bfloat16)
    return (residual_out, key_head, value_head)


def solution(mesh):
    return jax.shard_map(
        per_device,
        mesh=mesh,
        in_specs=(
            P(("seq", "head"), None),
            P(("seq", "head"), None),
            P(("seq", "head"), None),
            P(("seq", "head"), None),
            P(),
            P(),
            P("seq"),
            P(("seq", "head"), None),
            P(None, ("seq", "head")),
            P(None, ("seq", "head")),
            P(None, ("seq", "head")),
            P("head", None),
        ),
        out_specs=(P(("seq", "head"), None), P("seq", "head"), P("seq", "head")),
        check_vma=False,
    )
```

profile of v0, /device:TPU:0, one launch (start us, length us, event | category | flops | bytes accessed | tf_op | source)
XLA Modules:
  0.0 894.4 jit_solution(14546956432762249407)
XLA Ops:
  9.1 6.3 all-to-all-start
  21.9 3.3 all-to-all-start.1
  27.1 4.1 all-to-all-done.1
  36.5 88.6 %while.23 = (s32[]{:T(128)}, bf16[128,576]{1,0:T(8,128)(2,1)}, bf16[128,576]{1,0:T(8,128)(2,1)}, s32[128]{0:T(128)S(1)}, bf16[1024,576]{1,0:T(8,128)(2,1)}, /*in...) while((s32[]{:T(128)}, bf16[128,576]{1,0:T(8,128)(2,1)}, ...), condition=%wide.region_1.0_spmd, body=%wide.region_0.0_spmd.sunk | while | flops 7 | bytes 2396467 | solution.py:105
  37.8 4.1 collective-permute-start.1
  47.5 3.4 collective-permute-start
  50.9 4.2 collective-permute-start.1
  60.6 4.3 collective-permute-start
  64.9 4.2 collective-permute-start.1
  77.5 4.2 collective-permute-start.1
  90.1 4.2 collective-permute-start.1
  102.7 4.2 collective-permute-start.1
  115.3 4.2 collective-permute-start.1
  131.8 5.3 fusion.41
  144.2 21.1 %reduce-scatter.2.cloned.1.call-done = bf16[32,2304]{1,0:T(8,128)(2,1)} async-done(((bf16[128,2304]{1,0:T(8,128)(2,1)}), bf16[32,2304]{1,0:T(8,128)(2,1)}) %reduce-scatter.2.cloned.1.call-update) | async-done | bytes 147472 | tf_op jit(solution)/shard_map/reduce_scatter | solution.py:132
  167.7 3.8 all-to-all-start.3
  173.3 8.6 all-to-all-done.3
  182.1 212.7 %all-gather.4.cloned.1.call-done = bf16[2304,2880]{0,1:T(8,128)(2,1)} async-done(((bf16[2304,720]{0,1:T(8,128)(2,1)}), bf16[2304,2880]{0,1:T(8,128)(2,1)}) %all-gather.4.cloned.1.call-update) | async-done | bytes 13271056 | tf_op jit(solution)/shard_map/all_gather | solution.py:56
  394.8 8.8 fusion.46
  403.7 220.4 %all-gather.6.cloned.1.call-done = bf16[2304,2880]{0,1:T(8,128)(2,1)} async-done(((bf16[2304,720]{0,1:T(8,128)(2,1)}), bf16[2304,2880]{0,1:T(8,128)(2,1)}) %all-gather.6.cloned.1.call-update) | async-done | bytes 13271056 | tf_op jit(solution)/shard_map/all_gather | solution.py:57
  624.1 229.1 %all-gather.8.cloned.1.call-done = bf16[2304,2880]{0,1:T(8,128)(2,1)} async-done(((bf16[2304,720]{0,1:T(8,128)(2,1)}), bf16[2304,2880]{0,1:T(8,128)(2,1)}) %all-gather.8.cloned.1.call-update) | async-done | bytes 13271056 | tf_op jit(solution)/shard_map/all_gather | solution.py:58
  853.2 14.9 %convolution_convert_fusion.1 = bf16[72,2304]{1,0:T(8,128)(2,1)S(1)} fusion(bf16[2304,2880]{0,1:T(8,128)(2,1)} %all-gather.8.cloned.1.call-done, bf16[72,2304]{1,0:T(8,128)(2,1)S(1)} %reshape.164, bf16[2304,2880]{0,1:T(8,128)(2,1)} %all-gather.6.cloned.1.call-done, f32[72,2880]{1,0:T(8,128)S(1)} %fusion.46), kind=kOutput, calls=%fused_computation.11 | convolution fusion | flops 1912439808 | bytes 28035072 | tf_op jit(solution)/shard_map/dot_general | solution.py:170
  869.0 3.7 all-to-all-start.4
  872.7 10.4 %all-to-all-done.4 = bf16[8,9,2304]{2,1,0:T(8,128)(2,1)S(1)} async-done(((bf16[8,9,2304]{2,1,0:T(8,128)(2,1)}), bf16[8,9,2304]{2,1,0:T(8,128)(2,1)S(1)}, u32[]{:S(2)}, u32[]{:S(2)}) %all-to-all-start.4) | async-done | bytes 331808 | tf_op jit(solution)/shard_map/all_to_all | solution.py:173
  (148 shorter events, 90.9 us)
Async XLA Ops:
  9.1 12.7 %all-to-all-start = ((bf16[32,4,576]{2,0,1:T(8,128)(2,1)}), bf16[32,4,576]{2,0,1:T(8,128)(2,1)S(1)}, u32[]{:S(2)}, u32[]{:S(2)}) async-start(bf16[32,4,576]{2,0,1:T(8,128)(2,1)} %copy.57), calls=%async_computation | async-start | bytes 327680 | tf_op jit(solution)/shard_map/all_to_all | solution.py:71
  21.9 9.3 %all-to-all-start.1 = ((bf16[32,4,576]{2,0,1:T(8,128)(2,1)}), bf16[32,4,576]{2,0,1:T(8,128)(2,1)S(1)}, u32[]{:S(2)}, u32[]{:S(2)}) async-start(bf16[32,4,576]{2,0,1:T(8,128)(2,1)} %copy.58), calls=%async_computation.1 | async-start | bytes 327680 | tf_op jit(solution)/shard_map/all_to_all | solution.py:78
  31.2 96.2 %all-to-all-start.2 = ((bf16[32,4,576]{2,0,1:T(8,128)(2,1)}), bf16[32,4,576]{2,0,1:T(8,128)(2,1)S(1)}, u32[]{:S(2)}, u32[]{:S(2)}) async-start(bf16[32,4,576]{2,0,1:T(8,128)(2,1)} %copy.61), calls=%async_computation.2 | async-start | bytes 327680 | tf_op jit(solution)/shard_map/all_to_all | solution.py:64
  34.6 130.7 %reduce-scatter.2.cloned.1.call-start = ((), (), s32[]{:S(2)}) async-start(), calls=%async_computation.6 | async-start | bytes 737280 | tf_op jit(solution)/shard_map/reduce_scatter | solution.py:132
  36.5 8.3 collective-permute-start
  37.8 8.4 collective-permute-start.1
  41.9 2.7 collective-permute-start.2
  47.5 10.5 %collective-permute-start = (bf16[128,576]{1,0:T(8,128)(2,1)}, bf16[128,576]{1,0:T(8,128)(2,1)S(1)}, u32[]{:S(2)}, u32[]{:S(2)}) collective-permute-start(bf16[128,576]{1,0:T(8,128)(2,1)} %get-tuple-element.230), channel_id=1, source_target_pairs={{0,4},{4,8},{8,12},{12,16},{16,20},{20,24},{24,28},{1,5},{5,9},{9,... | collective-permute-start | bytes 442376 | tf_op jit(solution)/shard_map/while/body/eval_jaxpr/ppermute | solution.py:18
  50.9 8.4 collective-permute-start.1
  60.6 11.4 %collective-permute-start = (bf16[128,576]{1,0:T(8,128)(2,1)}, bf16[128,576]{1,0:T(8,128)(2,1)S(1)}, u32[]{:S(2)}, u32[]{:S(2)}) collective-permute-start(bf16[128,576]{1,0:T(8,128)(2,1)} %get-tuple-element.230), channel_id=1, source_target_pairs={{0,4},{4,8},{8,12},{12,16},{16,20},{20,24},{24,28},{1,5},{5,9},{9,... | collective-permute-start | bytes 442376 | tf_op jit(solution)/shard_map/while/body/eval_jaxpr/ppermute | solution.py:18
  64.9 8.4 collective-permute-start.1
  74.7 9.9 %collective-permute-start = (bf16[128,576]{1,0:T(8,128)(2,1)}, bf16[128,576]{1,0:T(8,128)(2,1)S(1)}, u32[]{:S(2)}, u32[]{:S(2)}) collective-permute-start(bf16[128,576]{1,0:T(8,128)(2,1)} %get-tuple-element.230), channel_id=1, source_target_pairs={{0,4},{4,8},{8,12},{12,16},{16,20},{20,24},{24,28},{1,5},{5,9},{9,... | collective-permute-start | bytes 442376 | tf_op jit(solution)/shard_map/while/body/eval_jaxpr/ppermute | solution.py:18
  77.5 8.4 collective-permute-start.1
  87.3 9.9 %collective-permute-start = (bf16[128,576]{1,0:T(8,128)(2,1)}, bf16[128,576]{1,0:T(8,128)(2,1)S(1)}, u32[]{:S(2)}, u32[]{:S(2)}) collective-permute-start(bf16[128,576]{1,0:T(8,128)(2,1)} %get-tuple-element.230), channel_id=1, source_target_pairs={{0,4},{4,8},{8,12},{12,16},{16,20},{20,24},{24,28},{1,5},{5,9},{9,... | collective-permute-start | bytes 442376 | tf_op jit(solution)/shard_map/while/body/eval_jaxpr/ppermute | solution.py:18
  90.1 8.4 collective-permute-start.1
  99.8 9.9 %collective-permute-start = (bf16[128,576]{1,0:T(8,128)(2,1)}, bf16[128,576]{1,0:T(8,128)(2,1)S(1)}, u32[]{:S(2)}, u32[]{:S(2)}) collective-permute-start(bf16[128,576]{1,0:T(8,128)(2,1)} %get-tuple-element.230), channel_id=1, source_target_pairs={{0,4},{4,8},{8,12},{12,16},{16,20},{20,24},{24,28},{1,5},{5,9},{9,... | collective-permute-start | bytes 442376 | tf_op jit(solution)/shard_map/while/body/eval_jaxpr/ppermute | solution.py:18
  102.7 8.4 collective-permute-start.1
  112.5 9.9 %collective-permute-start = (bf16[128,576]{1,0:T(8,128)(2,1)}, bf16[128,576]{1,0:T(8,128)(2,1)S(1)}, u32[]{:S(2)}, u32[]{:S(2)}) collective-permute-start(bf16[128,576]{1,0:T(8,128)(2,1)} %get-tuple-element.230), channel_id=1, source_target_pairs={{0,4},{4,8},{8,12},{12,16},{16,20},{20,24},{24,28},{1,5},{5,9},{9,... | collective-permute-start | bytes 442376 | tf_op jit(solution)/shard_map/while/body/eval_jaxpr/ppermute | solution.py:18
  115.3 8.4 collective-permute-start.1
  141.2 253.6 %all-gather.4.cloned.1.call-start = ((), (), s32[]{:S(2)}) async-start(), calls=%async_computation.7 | async-start | bytes 16588800 | tf_op jit(solution)/shard_map/all_gather | solution.py:56
  142.0 482.1 %all-gather.6.cloned.1.call-start = ((), (), s32[]{:S(2)}) async-start(), calls=%async_computation.8 | async-start | bytes 16588800 | tf_op jit(solution)/shard_map/all_gather | solution.py:57
  142.7 710.4 %all-gather.8.cloned.1.call-start = ((), (), s32[]{:S(2)}) async-start(), calls=%async_computation.9 | async-start | bytes 16588800 | tf_op jit(solution)/shard_map/all_gather | solution.py:58
  167.7 14.2 %all-to-all-start.3 = ((bf16[8,9,2304]{2,1,0:T(8,128)(2,1)}), bf16[8,9,2304]{2,1,0:T(8,128)(2,1)S(1)}, u32[]{:S(2)}, u32[]{:S(2)}) async-start(bf16[8,9,2304]{2,1,0:T(8,128)(2,1)} %reshape_broadcast_in_dim_reshape.3), calls=%async_computation.4 | async-start | bytes 1179648 | tf_op jit(solution)/shard_map/all_to_all | solution.py:164
  869.0 14.1 %all-to-all-start.4 = ((bf16[8,9,2304]{2,1,0:T(8,128)(2,1)}), bf16[8,9,2304]{2,1,0:T(8,128)(2,1)S(1)}, u32[]{:S(2)}, u32[]{:S(2)}) async-start(bf16[8,9,2304]{2,1,0:T(8,128)(2,1)} %reshape.165), calls=%async_computation.5 | async-start | bytes 1179648 | tf_op jit(solution)/shard_map/all_to_all | solution.py:173
  (14 other events, 256.6 us)
Sparse Core Ops, SparseCore 0:
  141.3 23.9 reduce-scatter.1
  166.9 227.8 all-gather.3
  396.4 227.6 all-gather.5
  625.5 227.6 all-gather.7
where the time goes:
time: 896 us; the launch traced here: 894 us
  waiting for transfers between devices  716 us (80%)
  starting transfers between devices  83.3 us (9%)
  local copies, waits for them, and re-layouts  42.8 us (5%)
  matrix products  33.7 us (4%)
  between operations  14 us (2%)
    all_gather x1, waiting for transfers between devices, per_device(): lax.all_gather(down_weight, 'head', axis=1, tiled=True)  229 us
    all_gather x1, waiting for transfers between devices, per_device(): lax.all_gather(up_weight, 'head', axis=1, tiled=True)  220 us
    all_gather x1, waiting for transfers between devices, per_device(): lax.all_gather(gate_weight, 'head', axis=1, tiled=True)  213 us
    ppermute x21, starting transfers between devices, passed_along(): return lax.ppermute(value, axis, pairs)  62.7 us
    reduce_scatter x1, waiting for transfers between devices, per_device(): lax.psum_scatter(jnp.dot(attention, out_weight, preferred_element_type=jn...  21.1 us
  transfers between devices with their start and end apart: 30, of which 15 were waited for; matrix products, arithmetic and copies ran while one was open for 5% of the time, Pallas kernels for 0%

commit v1 on v0

--- a/solution.py
+++ b/solution.py
@@ -1,3 +1,4 @@
+import functools
 import math
 import jax
 import jax.numpy as jnp
@@ -10,6 +11,22 @@
 CAP = 9
 residual_scale = 1.4 / math.sqrt(40.0)
 norm_epsilon = 1e-05
+
+
+def waves_view(x_local, a_name):
+    slots = lax.axis_size(a_name)
+    chunks = tuple(((tick, (tick + 1) % slots) for tick in range(slots)))
+    series = tuple(((tick, (tick - 1) % slots) for tick in range(slots)))
+    block_next, opened = ([x_local], [x_local])
+    for _ in range(slots // 2):
+        block_next.append(lax.ppermute(block_next[-1], axis_name=a_name, perm=chunks))
+    for _ in range((slots - 1) // 2):
+        opened.append(lax.ppermute(opened[-1], axis_name=a_name, perm=series))
+    formed = jnp.concatenate([*block_next[::-1], *opened[1:]], axis=1)
+    return jnp.roll(formed, (lax.axis_index(a_name) - slots // 2) * x_local.shape[1], axis=1)
+
+
+fit_outputs = functools.partial(waves_view, a_name="head")
 
 
 def passed_along(value, axis, by):
@@ -53,7 +70,7 @@
     stretch_len = tok_local * head_count
     span_count = min(2**LEVELS * 32 // tok_local, seq_count)
     gate_full, up_full, down_full = (
-        lax.all_gather(gate_weight, "head", axis=1, tiled=True),
+        fit_outputs(gate_weight),
         lax.all_gather(up_weight, "head", axis=1, tiled=True),
         lax.all_gather(down_weight, "head", axis=1, tiled=True),
     )

time: 896 us -> 855 us (0.954)
  waiting for transfers between devices: 716 us -> 596 us
  starting transfers between devices: 83.3 us -> 132 us
  local copies, waits for them, and re-layouts: 42.8 us -> 72.3 us
    ppermute x0 -> x3, waiting for transfers between devices: none -> 366 us  [the longest x2 248 us: waves_view(): lax.ppermute(block_next[-1], axis_name=a_name, perm=chunks)]
    all_gather x1, waiting for transfers between devices: 220 us -> 0.01 us  [per_device(): lax.all_gather(up_weight, 'head', axis=1, tiled=True)]
    all_gather x1 -> x0, waiting for transfers between devices: 213 us -> none  [per_device(): lax.all_gather(gate_weight, 'head', axis=1, tiled=True)]
    ppermute x0 -> x3, starting transfers between devices: none -> 46.3 us  [the longest x2 46.3 us: waves_view(): lax.ppermute(block_next[-1], axis_name=a_name, perm=chunks)]
    all_gather x1, waiting for transfers between devices: 229 us -> 198 us  [per_device(): lax.all_gather(down_weight, 'head', axis=1, tiled=True)]
    unnamed x21 -> x30, local copies, waits for them, and re-layouts: 3.05 us -> 27.3 us
    reduce_scatter x1, waiting for transfers between devices: 21.1 us -> 0.02 us  [per_device(): lax.psum_scatter(jnp.dot(attention, out_weight, preferred_element_type=jn...]
  transfers between devices with their start and end apart: 30 -> 32, of which waited for: 15 -> 15; matrix products, arithmetic and copies ran while one was open for 5% -> 9% of each run, Pallas kernels for 0% -> 0%
where the time goes in v1:
time: 855 us; the launch traced here: 853 us
  waiting for transfers between devices  596 us (70%)
  starting transfers between devices  132 us (15%)
  local copies, waits for them, and re-layouts  72.3 us (8%)
  matrix products  33.7 us (4%)
  between operations  14 us (2%)
    ppermute x2, waiting for transfers between devices, waves_view(): lax.ppermute(block_next[-1], axis_name=a_name, perm=chunks)  248 us
    all_gather x1, waiting for transfers between devices, per_device(): lax.all_gather(down_weight, 'head', axis=1, tiled=True)  198 us
    ppermute x1, waiting for transfers between devices, waves_view(): opened.append(lax.ppermute(opened[-1], axis_name=a_name, perm=series))  118 us
    ppermute x21, starting transfers between devices, passed_along(): return lax.ppermute(value, axis, pairs)  62.7 us
    ppermute x2, starting transfers between devices, waves_view(): lax.ppermute(block_next[-1], axis_name=a_name, perm=chunks)  46.3 us
    unnamed x30, local copies, waits for them, and re-layouts  27.3 us
  transfers between devices with their start and end apart: 32, of which 15 were waited for; matrix products, arithmetic and copies ran while one was open for 9% of the time, Pallas kernels for 0%

profile of v1, /device:TPU:0, one launch (start us, length us, event | category | flops | bytes accessed | tf_op | source)
XLA Modules:
  0.0 853.0 jit_solution(9249674297315324783)
XLA Ops:
  9.2 6.3 all-to-all-start
  36.5 88.7 %while.23 = (s32[]{:T(128)}, bf16[128,576]{1,0:T(8,128)(2,1)}, bf16[128,576]{1,0:T(8,128)(2,1)}, s32[128]{0:T(128)S(1)}, bf16[1024,576]{1,0:T(8,128)(2,1)}, /*in...) while((s32[]{:T(128)}, bf16[128,576]{1,0:T(8,128)(2,1)}, ...), condition=%wide.region_1.2_spmd, body=%wide.region_0.1_spmd.sunk | while | flops 7 | bytes 2396467 | solution.py:122
  37.8 4.1 collective-permute-start.1
  50.9 4.2 collective-permute-start.1
  60.7 4.3 collective-permute-start
  65.0 4.2 collective-permute-start.1
  77.6 4.2 collective-permute-start.1
  90.2 4.2 collective-permute-start.1
  102.8 4.2 collective-permute-start.1
  115.5 4.2 collective-permute-start.1
  132.0 5.3 fusion.48
  144.9 124.4 %collective-permute-done.3 = bf16[2304,720]{0,1:T(8,128)(2,1)} collective-permute-done((bf16[2304,720]{0,1:T(8,128)(2,1)}, bf16[2304,720]{0,1:T(8,128)(2,1)}, u32[]{:S(2)}, u32[]{:S(2)}) %collective-permute-start.3) | collective-permute-done | bytes 3317792 | tf_op jit(solution)/shard_map/ppermute | solution.py:22
  269.2 44.3 %collective-permute-start.4 = (bf16[2304,720]{0,1:T(8,128)(2,1)}, bf16[2304,720]{0,1:T(8,128)(2,1)}, u32[]{:S(2)}, u32[]{:S(2)}) collective-permute-start(bf16[2304,720]{0,1:T(8,128)(2,1)} %collective-permute-done.3), channel_id=1, source_target_pairs={{0,1},{1,2},{2,3},{3,0},{4,5},{5,6},{6,7},{7,4},{8,9},{9,10},{10,1... | collective-permute-start | bytes 9953288 | tf_op jit(solution)/shard_map/ppermute | solution.py:22
  316.8 6.0 all-to-all-start.3
  324.6 8.6 %all-to-all-done.3 = bf16[8,9,2304]{2,1,0:T(8,128)(2,1)S(1)} async-done(((bf16[8,9,2304]{2,1,0:T(8,128)(2,1)}), bf16[8,9,2304]{2,1,0:T(8,128)(2,1)S(1)}, u32[]{:S(2)}, u32[]{:S(2)}) %all-to-all-start.3) | async-done | bytes 331808 | tf_op jit(solution)/shard_map/all_to_all | solution.py:181
  333.4 123.7 %collective-permute-done.4 = bf16[2304,720]{0,1:T(8,128)(2,1)} collective-permute-done((bf16[2304,720]{0,1:T(8,128)(2,1)}, bf16[2304,720]{0,1:T(8,128)(2,1)}, u32[]{:S(2)}, u32[]{:S(2)}) %collective-permute-start.4) | collective-permute-done | bytes 3317792 | tf_op jit(solution)/shard_map/ppermute | solution.py:22
  466.9 117.8 %collective-permute-done.5 = bf16[2304,720]{0,1:T(8,128)(2,1)} collective-permute-done((bf16[2304,720]{0,1:T(8,128)(2,1)}, bf16[2304,720]{0,1:T(8,128)(2,1)}, u32[]{:S(2)}, u32[]{:S(2)}) %collective-permute-start.5) | collective-permute-done | bytes 3317792 | tf_op jit(solution)/shard_map/ppermute | solution.py:24
  588.7 4.4 constant_dynamic-update-slice_fusion.5
  593.1 4.2 constant_dynamic-update-slice_fusion.4
  603.1 9.0 %fusion.53 = f32[72,2880]{1,0:T(8,128)S(1)} fusion(bf16[72,2304]{1,0:T(8,128)(2,1)S(1)} %reshape.164, bf16[2304,2880]{0,1:T(8,128)(2,1)} %all-gather.3.cloned.1.call-done), kind=kOutput, calls=%fused_computation.70 | convolution fusion | flops 955514880 | bytes 14432256 | tf_op jit(solution)/shard_map/dot_general | solution.py:185
  612.1 197.9 %all-gather.5.cloned.1.call-done = bf16[2304,2880]{0,1:T(8,128)(2,1)} async-done(((bf16[2304,720]{0,1:T(8,128)(2,1)}), bf16[2304,2880]{0,1:T(8,128)(2,1)}) %all-gather.5.cloned.1.call-update) | async-done | bytes 13271056 | tf_op jit(solution)/shard_map/all_gather | solution.py:75
  810.0 14.9 %convolution_convert_fusion.1 = bf16[72,2304]{1,0:T(8,128)(2,1)S(1)} fusion(bf16[2304,2880]{0,1:T(8,128)(2,1)} %all-gather.5.cloned.1.call-done, f32[72,2880]{1,0:T(8,128)S(1)} %fusion.53, bf16[72,2304]{1,0:T(8,128)(2,1)S(1)} %reshape.164, bf16[2304,5760]{0,1:T(8,128)(2,1)} %constant_dynamic-update-slice_fusion.2, s32[]{:T(128)S(6)} %select_n.45), kind=kOutput, calls=%fused_computation.11 | convolution fusion | flops 1912439808 | bytes 28035076 | tf_op jit(solution)/shard_map/dot_general | solution.py:187
  825.9 4.2 all-to-all-start.4
  830.1 10.4 %all-to-all-done.4 = bf16[8,9,2304]{2,1,0:T(8,128)(2,1)} async-done(((bf16[8,9,2304]{2,1,0:T(8,128)(2,1)}), bf16[8,9,2304]{2,1,0:T(8,128)(2,1)}, u32[]{:S(2)}, u32[]{:S(2)}) %all-to-all-start.4) | async-done | bytes 331808 | tf_op jit(solution)/shard_map/all_to_all | solution.py:190
  (161 shorter events, 124.1 us)
Async XLA Ops:
  9.2 12.7 %all-to-all-start = ((bf16[32,4,576]{2,0,1:T(8,128)(2,1)}), bf16[32,4,576]{2,0,1:T(8,128)(2,1)S(1)}, u32[]{:S(2)}, u32[]{:S(2)}) async-start(bf16[32,4,576]{2,0,1:T(8,128)(2,1)} %copy.57), calls=%async_computation | async-start | bytes 327680 | tf_op jit(solution)/shard_map/all_to_all | solution.py:88
  21.9 9.3 %all-to-all-start.1 = ((bf16[32,4,576]{2,0,1:T(8,128)(2,1)}), bf16[32,4,576]{2,0,1:T(8,128)(2,1)S(1)}, u32[]{:S(2)}, u32[]{:S(2)}) async-start(bf16[32,4,576]{2,0,1:T(8,128)(2,1)} %copy.58), calls=%async_computation.1 | async-start | bytes 327680 | tf_op jit(solution)/shard_map/all_to_all | solution.py:95
  31.2 96.4 %all-to-all-start.2 = ((bf16[32,4,576]{2,0,1:T(8,128)(2,1)}), bf16[32,4,576]{2,0,1:T(8,128)(2,1)S(1)}, u32[]{:S(2)}, u32[]{:S(2)}) async-start(bf16[32,4,576]{2,0,1:T(8,128)(2,1)} %copy.61), calls=%async_computation.2 | async-start | bytes 327680 | tf_op jit(solution)/shard_map/all_to_all | solution.py:81
  34.6 279.9 %reduce-scatter.2.cloned.1.call-start = ((), (), s32[]{:S(2)}) async-start(), calls=%async_computation.6 | async-start | bytes 737280 | tf_op jit(solution)/shard_map/reduce_scatter | solution.py:149
  37.8 8.4 collective-permute-start.1
  47.5 10.5 %collective-permute-start = (bf16[128,576]{1,0:T(8,128)(2,1)}, bf16[128,576]{1,0:T(8,128)(2,1)S(1)}, u32[]{:S(2)}, u32[]{:S(2)}) collective-permute-start(bf16[128,576]{1,0:T(8,128)(2,1)} %get-tuple-element.230), channel_id=1, source_target_pairs={{0,4},{4,8},{8,12},{12,16},{16,20},{20,24},{24,28},{1,5},{5,9},{9,... | collective-permute-start | bytes 442376 | tf_op jit(solution)/shard_map/while/body/eval_jaxpr/ppermute | solution.py:35
  50.9 8.4 collective-permute-start.1
  60.7 11.4 %collective-permute-start = (bf16[128,576]{1,0:T(8,128)(2,1)}, bf16[128,576]{1,0:T(8,128)(2,1)S(1)}, u32[]{:S(2)}, u32[]{:S(2)}) collective-permute-start(bf16[128,576]{1,0:T(8,128)(2,1)} %get-tuple-element.230), channel_id=1, source_target_pairs={{0,4},{4,8},{8,12},{12,16},{16,20},{20,24},{24,28},{1,5},{5,9},{9,... | collective-permute-start | bytes 442376 | tf_op jit(solution)/shard_map/while/body/eval_jaxpr/ppermute | solution.py:35
  65.0 8.4 collective-permute-start.1
  74.7 9.9 %collective-permute-start = (bf16[128,576]{1,0:T(8,128)(2,1)}, bf16[128,576]{1,0:T(8,128)(2,1)S(1)}, u32[]{:S(2)}, u32[]{:S(2)}) collective-permute-start(bf16[128,576]{1,0:T(8,128)(2,1)} %get-tuple-element.230), channel_id=1, source_target_pairs={{0,4},{4,8},{8,12},{12,16},{16,20},{20,24},{24,28},{1,5},{5,9},{9,... | collective-permute-start | bytes 442376 | tf_op jit(solution)/shard_map/while/body/eval_jaxpr/ppermute | solution.py:35
  77.6 8.4 collective-permute-start.1
  87.4 9.9 %collective-permute-start = (bf16[128,576]{1,0:T(8,128)(2,1)}, bf16[128,576]{1,0:T(8,128)(2,1)S(1)}, u32[]{:S(2)}, u32[]{:S(2)}) collective-permute-start(bf16[128,576]{1,0:T(8,128)(2,1)} %get-tuple-element.230), channel_id=1, source_target_pairs={{0,4},{4,8},{8,12},{12,16},{16,20},{20,24},{24,28},{1,5},{5,9},{9,... | collective-permute-start | bytes 442376 | tf_op jit(solution)/shard_map/while/body/eval_jaxpr/ppermute | solution.py:35
  90.2 8.4 collective-permute-start.1
  100.0 9.9 %collective-permute-start = (bf16[128,576]{1,0:T(8,128)(2,1)}, bf16[128,576]{1,0:T(8,128)(2,1)S(1)}, u32[]{:S(2)}, u32[]{:S(2)}) collective-permute-start(bf16[128,576]{1,0:T(8,128)(2,1)} %get-tuple-element.230), channel_id=1, source_target_pairs={{0,4},{4,8},{8,12},{12,16},{16,20},{20,24},{24,28},{1,5},{5,9},{9,... | collective-permute-start | bytes 442376 | tf_op jit(solution)/shard_map/while/body/eval_jaxpr/ppermute | solution.py:35
  102.8 8.4 collective-permute-start.1
  112.6 9.9 %collective-permute-start = (bf16[128,576]{1,0:T(8,128)(2,1)}, bf16[128,576]{1,0:T(8,128)(2,1)S(1)}, u32[]{:S(2)}, u32[]{:S(2)}) collective-permute-start(bf16[128,576]{1,0:T(8,128)(2,1)} %get-tuple-element.230), channel_id=1, source_target_pairs={{0,4},{4,8},{8,12},{12,16},{16,20},{20,24},{24,28},{1,5},{5,9},{9,... | collective-permute-start | bytes 442376 | tf_op jit(solution)/shard_map/while/body/eval_jaxpr/ppermute | solution.py:35
  115.5 8.4 collective-permute-start.1
  141.4 461.7 %all-gather.3.cloned.1.call-start = ((), (), s32[]{:S(2)}) async-start(), calls=%async_computation.7 | async-start | bytes 16588800 | tf_op jit(solution)/shard_map/all_gather | solution.py:74
  142.2 667.8 %all-gather.5.cloned.1.call-start = ((), (), s32[]{:S(2)}) async-start(), calls=%async_computation.8 | async-start | bytes 16588800 | tf_op jit(solution)/shard_map/all_gather | solution.py:75
  142.9 126.3 %collective-permute-start.3 = (bf16[2304,720]{0,1:T(8,128)(2,1)}, bf16[2304,720]{0,1:T(8,128)(2,1)}, u32[]{:S(2)}, u32[]{:S(2)}) collective-permute-start(bf16[2304,720]{0,1:T(8,128)(2,1)} %param.22), channel_id=1, source_target_pairs={{0,1},{1,2},{2,3},{3,0},{4,5},{5,6},{6,7},{7,4},{8,9},{9,10},{10,1... | collective-permute-start | bytes 9953288 | tf_op jit(solution)/shard_map/ppermute | solution.py:22
  269.2 187.9 %collective-permute-start.4 = (bf16[2304,720]{0,1:T(8,128)(2,1)}, bf16[2304,720]{0,1:T(8,128)(2,1)}, u32[]{:S(2)}, u32[]{:S(2)}) collective-permute-start(bf16[2304,720]{0,1:T(8,128)(2,1)} %collective-permute-done.3), channel_id=1, source_target_pairs={{0,1},{1,2},{2,3},{3,0},{4,5},{5,6},{6,7},{7,4},{8,9},{9,10},{10,1... | collective-permute-start | bytes 9953288 | tf_op jit(solution)/shard_map/ppermute | solution.py:22
  313.5 271.2 %collective-permute-start.5 = (bf16[2304,720]{0,1:T(8,128)(2,1)}, bf16[2304,720]{0,1:T(8,128)(2,1)}, u32[]{:S(2)}, u32[]{:S(2)}) collective-permute-start(bf16[2304,720]{0,1:T(8,128)(2,1)} %param.22), channel_id=1, source_target_pairs={{0,3},{1,0},{2,1},{3,2},{4,7},{5,4},{6,5},{7,6},{8,11},{9,8},{10,9... | collective-permute-start | bytes 9953288 | tf_op jit(solution)/shard_map/ppermute | solution.py:24
  316.8 16.4 %all-to-all-start.3 = ((bf16[8,9,2304]{2,1,0:T(8,128)(2,1)}), bf16[8,9,2304]{2,1,0:T(8,128)(2,1)S(1)}, u32[]{:S(2)}, u32[]{:S(2)}) async-start(bf16[8,9,2304]{2,1,0:T(8,128)(2,1)} %reshape_broadcast_in_dim_reshape.3), calls=%async_computation.4 | async-start | bytes 1179648 | tf_op jit(solution)/shard_map/all_to_all | solution.py:181
  825.9 14.7 %all-to-all-start.4 = ((bf16[8,9,2304]{2,1,0:T(8,128)(2,1)}), bf16[8,9,2304]{2,1,0:T(8,128)(2,1)}, u32[]{:S(2)}, u32[]{:S(2)}) async-start(bf16[8,9,2304]{2,1,0:T(8,128)(2,1)} %reshape.165), calls=%async_computation.5 | async-start | bytes 1179648 | tf_op jit(solution)/shard_map/all_to_all | solution.py:190
  (17 other events, 906.9 us)
Sparse Core Ops, SparseCore 0:
  141.5 31.7 reduce-scatter.1
  174.8 404.1 all-gather.2
  580.6 229.3 all-gather.4
